TPU v7x, 512 devices: a whole 4x8x8 slice. The times are simulated.
512 devices in a mesh: context: 32 (over x_hi, y, core), tensor: 16 (over z, x_lo).
Axes of the slice: x: 4 (x_hi: 2, x_lo: 2; x = x_hi * 2 + x_lo), y: 8, z: 8, core: 2. Of those that a mesh axis runs over, the one named last changes fastest.
Arguments:
- projected: bfloat16 [3, 12288, 8192], P(None, 'context', 'tensor'), may hold values from -6 to 6
- taps: float32 [3, 3, 8192], P(None, None, 'tensor'), may hold values from -4 to 4
- filters: bfloat16 [512, 128], P('tensor'), may hold values from -0.5 to 0.5
- skip: float32 [8192], P('tensor'), may hold values from -4 to 4
- out_weight: bfloat16 [8192, 8192], P('tensor', 'context'), may hold values from -0.125 to 0.125
- positions: int32 [128], replicated, may hold values from 0 to 12287
Outputs:
- mixed: bfloat16 [12288, 8192], P('context', 'tensor')
- variant_states: bfloat16 [128, 8192], P('context', 'tensor')
All inputs are finite; a program needn't handle non-finite values.
Results may differ from a plain program's by a relative error of at most 0.018.
Values may be sent and summed in bfloat16 or wider, within the bound.
No kernel may reach another device: no remote copies, remote signals or barrier semaphores. Data moves between devices by JAX's collectives and lax.ppermute only.
A program may use at most 128 MiB of HBM per device.

v0:
```python
import jax
import jax.numpy as jnp
from jax import lax
import numpy as np
from jax.sharding import Mesh, PartitionSpec as P

FLT = 128
GROUP = 16
SHORT = 3


def shifted(array, axis, by):
    size = lax.axis_size(axis)
    pairs = [(i, i + by) for i in range(size) if 0 <= i + by < size]
    return lax.ppermute(array, axis, pairs)


def pair_scatter(block, axis):
    me = lax.axis_index(axis)
    half = block.shape[1] // 2
    keep = lax.dynamic_slice_in_dim(block, me * half, half, 1)
    send = lax.dynamic_slice_in_dim(block, (1 - me) * half, half, 1)
    got = lax.ppermute(send, axis, [(0, 1), (1, 0)])
    return (keep.astype(jnp.float32) + got.astype(jnp.float32)).astype(block.dtype)


def exchange_scatter(rows, axis):
    size = lax.axis_size(axis)
    pieces = rows.reshape(size, rows.shape[0] // size, rows.shape[1])
    pieces = lax.all_to_all(pieces, axis, 0, 0, tiled=True)
    return pieces.astype(jnp.float32).sum(0).astype(rows.dtype)


def short_filter(extended, weights, count):
    lags = SHORT - 1
    total = jnp.zeros((extended.shape[0], count, extended.shape[2]), jnp.float32)
    for lag in range(SHORT):
        total = total + weights[:, lag, None, :] * extended[
            :, lags - lag : lags - lag + count, :
        ].astype(jnp.float32)
    return total


def banded_filters(filters, rows):
    local_groups = filters.shape[0]
    span = FLT - 1 + rows
    reversed_taps = jnp.flip(filters, axis=1)
    padded_taps = jnp.concatenate(
        [reversed_taps, jnp.zeros((local_groups, rows), filters.dtype)], axis=1
    )
    tiled = jnp.tile(padded_taps, (1, rows))
    return tiled[:, : rows * span].reshape(local_groups, rows, span)


def on_device(projected, taps, filters, skip, out_weight, positions):
    rows = projected.shape[1]
    width = projected.shape[2]
    lags = SHORT - 1
    reach = FLT - 1
    rim = shifted(projected[:, rows - lags :, :], "context", 1)
    feat = short_filter(jnp.concatenate([rim, projected], axis=1), taps, rows)
    query = feat[0]
    product = (feat[1] * feat[2]).astype(jnp.bfloat16)
    prior = shifted(product[rows - reach :], "context", 1)
    extended = jnp.concatenate([prior, product], axis=0)
    span = reach + rows
    toeplitz = banded_filters(filters, rows)
    local_groups = filters.shape[0]
    conv = jnp.einsum(
        "gim,mgc->igc",
        toeplitz,
        extended.reshape(span, local_groups, GROUP),
        preferred_element_type=jnp.float32,
    ).reshape(rows, width)
    conv = conv + skip[None, :] * product.astype(jnp.float32)
    gated = lax.optimization_barrier((query * conv).astype(jnp.bfloat16))
    offset = lax.axis_index("context") * rows
    local_sites = positions - offset
    one_hot = (local_sites[:, None] == jnp.arange(rows, dtype=jnp.int32)[None, :]).astype(
        jnp.bfloat16
    )
    picked_gated = jnp.dot(one_hot, gated, preferred_element_type=jnp.float32)
    site_gated = exchange_scatter(picked_gated.astype(jnp.bfloat16), "context")
    gated, site_gated = lax.optimization_barrier((gated, site_gated))
    full_weight = lax.all_gather(out_weight, "context", axis=1, tiled=True)
    sites = site_gated.shape[0]
    padding = jnp.zeros((-(rows + sites) % 8, width), gated.dtype)
    both = lax.optimization_barrier(jnp.concatenate([gated, site_gated, padding], axis=0))
    both = jnp.dot(both, full_weight, preferred_element_type=jnp.float32).astype(jnp.bfloat16)
    partial = lax.psum_scatter(both, "z", scatter_dimension=1, tiled=True)
    reduced = pair_scatter(partial, "x_lo")
    mixed = reduced[:rows]
    variant_states = reduced[rows : rows + sites]
    return (mixed, variant_states)


def split_mesh(mesh):
    devices = np.asarray(mesh.devices)
    context, tensor = devices.shape
    return Mesh(devices.reshape(context, tensor // 2, 2), ("context", "z", "x_lo"))


def solution(mesh):
    tensor = ("z", "x_lo")
    return jax.shard_map(
        on_device,
        mesh=split_mesh(mesh),
        in_specs=(
            P(None, "context", tensor),
            P(None, None, tensor),
            P(tensor, None),
            P(tensor),
            P(tensor, "context"),
            P(),
        ),
        out_specs=(P("context", tensor), P("context", tensor)),
        check_vma=False,
    )
```

profile of v0, /device:TPU:1, one launch (start us, length us, event | category | flops | bytes accessed | tf_op | source)
XLA Modules:
  0.0 241.7 jit_solution(7688944672993362209)
XLA Ops:
  7.2 0.0 all-gather.2.cloned.1.call-start
  7.2 0.7 all-gather.2.cloned.1.call-update
  7.9 0.8 slice.44
  8.7 4.6 %collective-permute-start = (bf16[3,2,512]{2,1,0:T(2,128)(2,1)S(1)}, bf16[3,2,512]{2,1,0:T(2,128)(2,1)S(1)}, u32[]{:S(2)}, u32[]{:S(2)}) collective-permute-start(bf16[3,2,512]{2,1,0:T(2,128)(2,1)S(1)} %slice.44), channel_id=1, source_target_pairs={{0,16},{16,32},{32,48},{48,64},{64,80},{80,96},{96,112},{112,128},... | collective-permute-start | bytes 18440 | tf_op jit(solution)/shard_map/ppermute | solution.py:15
  13.3 0.9 fusion.5
  14.1 1.2 broadcast_subtract_fusion
  15.3 0.6 copy.19
  15.9 0.8 rev.4
  16.7 5.4 %tile.4 = bf16[32,384,512]{2,1,0:T(8,128)(2,1)} broadcast(bf16[32,512]{1,0:T(8,128)(2,1)S(1)} %concatenate.14), dimensions={0,2} | broadcast | bytes 12615680 | tf_op jit(solution)/shard_map/tile | solution.py:51
  22.1 12.0 %copy.15 = bf16[4,8,384,512]{3,1,2,0:T(8,128)(2,1)S(1)} copy(bf16[4,8,384,512]{3,2,1,0:T(8,128)(2,1)} %bitcast.29) | data formatting | bytes 25165824
  34.2 5.2 %slice.62 = bf16[32,196224]{1,0:T(8,128)(2,1)} slice(bf16[32,196608]{1,0:T(8,128)(2,1)S(1)} %bitcast.30), slice={[0:32], [0:196224]} | slice | bytes 25116672 | tf_op jit(solution)/shard_map/slice | solution.py:52
  39.3 0.0 copy-start
  39.3 29.3 %reshape.26 = bf16[32,384,511]{2,1,0:T(8,128)(2,1)} reshape(bf16[32,196224]{1,0:T(8,128)(2,1)} %slice.62) | data formatting | bytes 25116672 | tf_op jit(solution)/shard_map/reshape | solution.py:52
  68.7 0.0 collective-permute-done
  68.7 0.0 copy-start.1
  68.7 0.6 copy-done.1
  69.3 0.0 copy-done
  69.3 1.5 multiply_add_fusion
  70.8 0.1 fusion.1
  71.0 2.1 collective-permute-start.1
  73.1 0.1 fusion.12
  73.2 3.4 %collective-permute-done.1 = bf16[127,512]{1,0:T(8,128)(2,1)S(1)} collective-permute-done((bf16[127,512]{1,0:T(8,128)(2,1)S(1)}, bf16[127,512]{1,0:T(8,128)(2,1)S(1)}, u32[]{:S(2)}, u32[]{:S(2)}) %collective-permute-start.1) | collective-permute-done | bytes 130080 | tf_op jit(solution)/shard_map/ppermute | solution.py:15
  76.6 0.1 pad_maximum_fusion.1
  76.7 0.2 copy.10
  76.9 0.0 copy-start.2
  76.9 9.0 %fusion.6 = f32[32,16,384]{2,1,0:T(8,128)} fusion(bf16[511,32,16]{0,2,1:T(8,128)(2,1)S(1)} %bitcast.32, bf16[32,384,511]{2,1,0:T(8,128)(2,1)} %reshape.26), kind=kOutput, calls=%fused_computation.24 | convolution fusion | flops 200933376 | bytes 13868032 | tf_op jit(solution)/shard_map/gim,mgc->igc/dot_general | solution.py:69
  86.0 0.0 copy-start.3
  86.0 1.4 copy.11
  87.4 0.0 copy-done.2
  87.4 0.4 fusion.3
  87.8 0.0 copy-done.3
  87.8 0.3 convolution_convert_fusion.1
  88.1 0.7 reshape.28
  88.8 12.8 %all-to-all-start = ((bf16[32,4,512]{2,1,0:T(4,128)(2,1)}), bf16[32,4,512]{2,1,0:T(4,128)(2,1)S(1)}, u32[]{:S(2)}, u32[]{:S(2)}) async-start(bf16[32,4,512]{2,1,0:T(4,128)(2,1)} %reshape.28), calls=%async_computation | async-start | bytes 262144 | tf_op jit(solution)/shard_map/all_to_all | solution.py:30
  101.5 0.0 reduce-scatter.2.cloned.1.call-start
  101.6 0.1 pad.3.clone
  101.7 10.8 %all-to-all-done = bf16[32,4,512]{2,1,0:T(4,128)(2,1)S(1)} async-done(((bf16[32,4,512]{2,1,0:T(4,128)(2,1)}), bf16[32,4,512]{2,1,0:T(4,128)(2,1)S(1)}, u32[]{:S(2)}, u32[]{:S(2)}) %all-to-all-start) | async-done | bytes 131104 | tf_op jit(solution)/shard_map/all_to_all | solution.py:30
  112.4 0.1 reduce_sum.12
  112.5 0.1 maximum_maximum_fusion
  112.6 20.2 %all-gather.2.cloned.1.call-done = bf16[512,8192]{1,0:T(8,128)(2,1)} async-done(((bf16[512,256]{1,0:T(8,128)(2,1)}), bf16[512,8192]{1,0:T(8,128)(2,1)}) %all-gather.2.cloned.1.call-update) | async-done | bytes 8388624 | tf_op jit(solution)/shard_map/all_gather | solution.py:85
  132.8 8.9 %convolution_convert_fusion = bf16[392,8192]{1,0:T(8,128)(2,1)} fusion(bf16[392,512]{1,0:T(8,128)(2,1)S(1)} %maximum_maximum_fusion, bf16[512,8192]{1,0:T(8,128)(2,1)} %all-gather.2.cloned.1.call-done), kind=kOutput, calls=%fused_computation | convolution fusion | flops 3291545600 | bytes 15212544 | tf_op jit(solution)/shard_map/dot_general | solution.py:89
  141.7 0.0 reduce-scatter.2.cloned.1.call-update
  141.7 77.5 %reduce-scatter.2.cloned.1.call-done = bf16[392,1024]{1,0:T(8,128)(2,1)} async-done(((bf16[392,8192]{1,0:T(8,128)(2,1)}), bf16[392,1024]{1,0:T(8,128)(2,1)}) %reduce-scatter.2.cloned.1.call-update) | async-done | bytes 802832 | tf_op jit(solution)/shard_map/reduce_scatter | solution.py:90
  219.2 1.0 constant_dynamic-slice_fusion
  220.3 3.1 %collective-permute-start.2 = (bf16[392,512]{1,0:T(8,128)(2,1)S(1)}, bf16[392,512]{1,0:T(8,128)(2,1)S(1)}, u32[]{:S(2)}, u32[]{:S(2)}) collective-permute-start(bf16[392,512]{1,0:T(8,128)(2,1)S(1)} %constant_dynamic-slice_fusion), channel_id=1, source_target_pairs={{0,1},{1,0},{2,3},{3,2},{4,5},{5,4},{6,7},{7,6},{8,9},{9,8},{10,11... | collective-permute-start | bytes 1204232 | tf_op jit(solution)/shard_map/ppermute | solution.py:23
  223.4 9.0 %collective-permute-done.2 = bf16[392,512]{1,0:T(8,128)(2,1)S(1)} collective-permute-done((bf16[392,512]{1,0:T(8,128)(2,1)S(1)}, bf16[392,512]{1,0:T(8,128)(2,1)S(1)}, u32[]{:S(2)}, u32[]{:S(2)}) %collective-permute-start.2) | collective-permute-done | bytes 401440 | tf_op jit(solution)/shard_map/ppermute | solution.py:23
  232.4 1.1 add_convert_fusion
  233.5 0.8 slice.63
  234.2 0.6 slice.64
  (4 shorter events, 0.1 us)
Async XLA Ops:
  7.2 125.6 %all-gather.2.cloned.1.call-start = ((), (), s32[]{:S(2)}) async-start(), calls=%async_computation.2 | async-start | bytes 8650752 | tf_op jit(solution)/shard_map/all_gather | solution.py:85
  8.7 60.0 %collective-permute-start = (bf16[3,2,512]{2,1,0:T(2,128)(2,1)S(1)}, bf16[3,2,512]{2,1,0:T(2,128)(2,1)S(1)}, u32[]{:S(2)}, u32[]{:S(2)}) collective-permute-start(bf16[3,2,512]{2,1,0:T(2,128)(2,1)S(1)} %slice.44), channel_id=1, source_target_pairs={{0,16},{16,32},{32,48},{48,64},{64,80},{80,96},{96,112},{112,128},... | collective-permute-start | bytes 18440 | tf_op jit(solution)/shard_map/ppermute | solution.py:15
  39.3 29.9 %copy-start = (bf16[3,384,512]{2,1,0:T(8,128)(2,1)S(1)}, bf16[3,384,512]{2,1,0:T(8,128)(2,1)}, u32[]{:S(2)}) copy-start(bf16[3,384,512]{2,1,0:T(8,128)(2,1)} %param.6) | copy-start | bytes 3538948
  68.7 0.6 copy-start.1
  71.0 5.7 %collective-permute-start.1 = (bf16[127,512]{1,0:T(8,128)(2,1)S(1)}, bf16[127,512]{1,0:T(8,128)(2,1)S(1)}, u32[]{:S(2)}, u32[]{:S(2)}) collective-permute-start(bf16[127,512]{1,0:T(8,128)(2,1)S(1)} %slice_bitcast_fusion.1), channel_id=1, source_target_pairs={{0,16},{16,32},{32,48},{48,64},{64,80},{80,96},{96,112},{112,128},... | collective-permute-start | bytes 390152 | tf_op jit(solution)/shard_map/ppermute | solution.py:15
  76.9 10.4 %copy-start.2 = (f32[512]{0:T(512)S(1)}, f32[512]{0:T(512)}, u32[]{:S(2)}) copy-start(f32[512]{0:T(512)} %param.9) | copy-start | bytes 6148
  86.0 1.8 copy-start.3
  88.8 23.7 %all-to-all-start = ((bf16[32,4,512]{2,1,0:T(4,128)(2,1)}), bf16[32,4,512]{2,1,0:T(4,128)(2,1)S(1)}, u32[]{:S(2)}, u32[]{:S(2)}) async-start(bf16[32,4,512]{2,1,0:T(4,128)(2,1)} %reshape.28), calls=%async_computation | async-start | bytes 262144 | tf_op jit(solution)/shard_map/all_to_all | solution.py:30
  101.5 117.7 %reduce-scatter.2.cloned.1.call-start = ((), (), s32[]{:S(2)}) async-start(), calls=%async_computation.3 | async-start | bytes 7225344 | tf_op jit(solution)/shard_map/reduce_scatter | solution.py:90
  220.3 12.1 %collective-permute-start.2 = (bf16[392,512]{1,0:T(8,128)(2,1)S(1)}, bf16[392,512]{1,0:T(8,128)(2,1)S(1)}, u32[]{:S(2)}, u32[]{:S(2)}) collective-permute-start(bf16[392,512]{1,0:T(8,128)(2,1)S(1)} %constant_dynamic-slice_fusion), channel_id=1, source_target_pairs={{0,1},{1,0},{2,3},{3,2},{4,5},{5,4},{6,7},{7,6},{8,9},{9,8},{10,11... | collective-permute-start | bytes 1204232 | tf_op jit(solution)/shard_map/ppermute | solution.py:23
Sparse Core Ops, SparseCore 0:
  11.1 121.6 all-gather.1
  141.8 77.3 reduce-scatter.1
where the time goes:
time: 242 us
  waiting for transfers between devices  122 us (50%)
  local copies, waits for them, and re-layouts  60.4 us (25%)
  starting transfers between devices  22.6 us (9%)
  matrix products  18.2 us (8%)
  between operations  14.2 us (6%)
  other arithmetic  4.73 us (2%)
    reduce_scatter x1, waiting for transfers between devices, on_device(): partial = lax.psum_scatter(both, 'z', scatter_dimension=1, tiled=True)  77.5 us
    reshape x1, local copies, waits for them, and re-layouts, banded_filters(): return tiled[:, :rows * span].reshape(local_groups, rows, span)  29.3 us
    all_gather x1, waiting for transfers between devices, on_device(): full_weight = lax.all_gather(out_weight, 'context', axis=1, tiled=True)  20.2 us
    unnamed x11, local copies, waits for them, and re-layouts  13.2 us
    all_to_all x1, starting transfers between devices, exchange_scatter(): pieces = lax.all_to_all(pieces, axis, 0, 0, tiled=True)  12.8 us
    all_to_all x1, waiting for transfers between devices, exchange_scatter(): pieces = lax.all_to_all(pieces, axis, 0, 0, tiled=True)  10.8 us
    dot_general x1, matrix products, on_device(): jnp.einsum('gim,mgc->igc', toeplitz, extended.reshape(span, local_groups,...  9.02 us
    ppermute x1, waiting for transfers between devices, pair_scatter(): got = lax.ppermute(send, axis, [(0, 1), (1, 0)])  9 us
  transfers between devices with their start and end apart: 6, of which 5 were waited for; matrix products, arithmetic and copies ran while one was open for 29% of the time, Pallas kernels for 0%

commit v1 on v0

--- a/solution.py
+++ b/solution.py
@@ -82,7 +82,9 @@
     picked_gated = jnp.dot(one_hot, gated, preferred_element_type=jnp.float32)
     site_gated = exchange_scatter(picked_gated.astype(jnp.bfloat16), "context")
     gated, site_gated = lax.optimization_barrier((gated, site_gated))
-    full_weight = lax.all_gather(out_weight, "context", axis=1, tiled=True)
+    full_weight = jnp.concatenate(
+        lax.all_to_all(jnp.stack([out_weight] * lax.axis_size("context")), "context", 0, 0), axis=1
+    )
     sites = site_gated.shape[0]
     padding = jnp.zeros((-(rows + sites) % 8, width), gated.dtype)
     both = lax.optimization_barrier(jnp.concatenate([gated, site_gated, padding], axis=0))

time: 242 us -> 423 us (1.75)
  waiting for transfers between devices: 122 us -> 292 us
  local copies, waits for them, and re-layouts: 60.4 us -> 65.6 us
    all_to_all x0 -> x1, waiting for transfers between devices: none -> 185 us  [on_device(): lax.all_to_all(jnp.stack([out_weight] * lax.axis_size('context')), 'conte...]
    all_gather x1 -> x0, waiting for transfers between devices: 20.2 us -> none  [on_device(): full_weight = lax.all_gather(out_weight, 'context', axis=1, tiled=True)]
    reduce_scatter x1, waiting for transfers between devices: 77.5 us -> 84.5 us  [on_device(): partial = lax.psum_scatter(both, 'z', scatter_dimension=1, tiled=True)]
    all_to_all x0 -> x1, starting transfers between devices: none -> 6.18 us  [on_device(): lax.all_to_all(jnp.stack([out_weight] * lax.axis_size('context')), 'conte...]
    unnamed x11 -> x12, local copies, waits for them, and re-layouts: 13.2 us -> 14.3 us
  transfers between devices with their start and end apart: 6 -> 6, of which waited for: 5 -> 5; matrix products, arithmetic and copies ran while one was open for 29% -> 13% of each run, Pallas kernels for 0% -> 0%
where the time goes in v1:
time: 423 us
  waiting for transfers between devices  292 us (69%)
  local copies, waits for them, and re-layouts  65.6 us (16%)
  starting transfers between devices  26.4 us (6%)
  matrix products  19.8 us (5%)
  between operations  14.2 us (3%)
  other arithmetic  4.73 us (1%)
    all_to_all x1, waiting for transfers between devices, on_device(): lax.all_to_all(jnp.stack([out_weight] * lax.axis_size('context')), 'conte...  185 us
    reduce_scatter x1, waiting for transfers between devices, on_device(): partial = lax.psum_scatter(both, 'z', scatter_dimension=1, tiled=True)  84.5 us
    reshape x1, local copies, waits for them, and re-layouts, banded_filters(): return tiled[:, :rows * span].reshape(local_groups, rows, span)  29.3 us
    unnamed x12, local copies, waits for them, and re-layouts  14.3 us
    dot_general x1, matrix products, on_device(): jnp.dot(both, full_weight, preferred_element_type=jnp.float32)  10.7 us
    all_to_all x1, starting transfers between devices, exchange_scatter(): pieces = lax.all_to_all(pieces, axis, 0, 0, tiled=True)  10.4 us
    all_to_all x1, waiting for transfers between devices, exchange_scatter(): pieces = lax.all_to_all(pieces, axis, 0, 0, tiled=True)  9.47 us
    ppermute x1, waiting for transfers between devices, pair_scatter(): got = lax.ppermute(send, axis, [(0, 1), (1, 0)])  8.99 us
  transfers between devices with their start and end apart: 6, of which 5 were waited for; matrix products, arithmetic and copies ran while one was open for 13% of the time, Pallas kernels for 0%

profile of v1, /device:TPU:1, one launch (start us, length us, event | category | flops | bytes accessed | tf_op | source)
XLA Modules:
  0.0 422.6 jit_solution(14449504668288775206)
XLA Ops:
  7.2 0.8 slice.44
  7.9 4.6 %collective-permute-start = (bf16[3,2,512]{2,1,0:T(2,128)(2,1)S(1)}, bf16[3,2,512]{2,1,0:T(2,128)(2,1)S(1)}, u32[]{:S(2)}, u32[]{:S(2)}) collective-permute-start(bf16[3,2,512]{2,1,0:T(2,128)(2,1)S(1)} %slice.44), channel_id=1, source_target_pairs={{0,16},{16,32},{32,48},{48,64},{64,80},{80,96},{96,112},{112,128},... | collective-permute-start | bytes 18440 | tf_op jit(solution)/shard_map/ppermute | solution.py:15
  12.5 0.9 fusion.5
  13.4 1.2 broadcast_subtract_fusion
  14.6 0.6 copy.20
  15.2 0.8 rev.4
  16.0 5.5 %tile.4 = bf16[32,384,512]{2,1,0:T(8,128)(2,1)} broadcast(bf16[32,512]{1,0:T(8,128)(2,1)S(1)} %concatenate.14), dimensions={0,2} | broadcast | bytes 12615680 | tf_op jit(solution)/shard_map/tile | solution.py:51
  21.5 12.0 %copy.16 = bf16[4,8,384,512]{3,1,2,0:T(8,128)(2,1)S(1)} copy(bf16[4,8,384,512]{3,2,1,0:T(8,128)(2,1)} %bitcast.32) | data formatting | bytes 25165824
  33.5 5.1 %slice.62 = bf16[32,196224]{1,0:T(8,128)(2,1)} slice(bf16[32,196608]{1,0:T(8,128)(2,1)S(1)} %bitcast.33), slice={[0:32], [0:196224]} | slice | bytes 25116672 | tf_op jit(solution)/shard_map/slice | solution.py:52
  38.6 0.0 copy-start
  38.6 29.3 %reshape.34 = bf16[32,384,511]{2,1,0:T(8,128)(2,1)} reshape(bf16[32,196224]{1,0:T(8,128)(2,1)} %slice.62) | data formatting | bytes 25116672 | tf_op jit(solution)/shard_map/reshape | solution.py:52
  67.9 0.0 collective-permute-done
  67.9 0.0 copy-start.1
  67.9 0.6 copy-done.1
  68.5 0.0 copy-done
  68.5 1.5 multiply_add_fusion
  70.1 0.1 fusion.1
  70.2 2.1 collective-permute-start.1
  72.3 0.1 fusion.12
  72.4 3.5 collective-permute-done.1
  75.9 0.1 pad_maximum_fusion.1
  76.0 0.2 copy.10
  76.2 0.0 copy-start.2
  76.2 8.9 %fusion.6 = f32[32,16,384]{2,1,0:T(8,128)} fusion(bf16[511,32,16]{0,2,1:T(8,128)(2,1)S(1)} %bitcast.35, bf16[32,384,511]{2,1,0:T(8,128)(2,1)} %reshape.34), kind=kOutput, calls=%fused_computation.24 | convolution fusion | flops 200933376 | bytes 13868032 | tf_op jit(solution)/shard_map/gim,mgc->igc/dot_general | solution.py:69
  85.1 0.0 copy-start.3
  85.1 1.4 copy.11
  86.5 0.0 copy-done.2
  86.5 0.4 fusion.3
  86.9 0.0 copy-done.3
  86.9 0.3 convolution_convert_fusion.1
  87.2 0.7 reshape.36
  87.9 10.4 %all-to-all-start = ((bf16[32,4,512]{2,1,0:T(4,128)(2,1)}), bf16[32,4,512]{2,1,0:T(4,128)(2,1)S(1)}, u32[]{:S(2)}, u32[]{:S(2)}) async-start(bf16[32,4,512]{2,1,0:T(4,128)(2,1)} %reshape.36), calls=%async_computation | async-start | bytes 262144 | tf_op jit(solution)/shard_map/all_to_all | solution.py:30
  98.3 1.1 copy.12
  99.4 9.5 %all-to-all-done = bf16[32,4,512]{2,1,0:T(4,128)(2,1)S(1)} async-done(((bf16[32,4,512]{2,1,0:T(4,128)(2,1)}), bf16[32,4,512]{2,1,0:T(4,128)(2,1)S(1)}, u32[]{:S(2)}, u32[]{:S(2)}) %all-to-all-start) | async-done | bytes 131104 | tf_op jit(solution)/shard_map/all_to_all | solution.py:30
  108.8 4.2 stack.2
  113.0 6.2 %all-to-all-start.1 = ((bf16[32,512,256]{1,2,0:T(8,128)(2,1)}), bf16[32,512,256]{1,2,0:T(8,128)(2,1)}, u32[]{:S(2)}, u32[]{:S(2)}) async-start(bf16[32,512,256]{1,2,0:T(8,128)(2,1)} %stack.2), calls=%async_computation.1 | async-start | bytes 16777216 | tf_op jit(solution)/shard_map/all_to_all | solution.py:86
  119.2 0.0 reduce-scatter.2.cloned.1.call-start
  119.3 0.1 pad.3.clone
  119.4 0.1 reduce_sum.12
  119.4 0.1 maximum_maximum_fusion
  119.6 185.3 %all-to-all-done.1 = bf16[32,512,256]{1,2,0:T(8,128)(2,1)} async-done(((bf16[32,512,256]{1,2,0:T(8,128)(2,1)}), bf16[32,512,256]{1,2,0:T(8,128)(2,1)}, u32[]{:S(2)}, u32[]{:S(2)}) %all-to-all-start.1) | async-done | bytes 8388640 | tf_op jit(solution)/shard_map/all_to_all | solution.py:86
  304.9 10.7 %convolution_convert_fusion = bf16[392,8192]{1,0:T(8,128)(2,1)} fusion(bf16[392,512]{1,0:T(8,128)(2,1)S(1)} %maximum_maximum_fusion, bf16[512,8192]{0,1:T(8,128)(2,1)} %bitcast.7), kind=kOutput, calls=%fused_computation | convolution fusion | flops 3291545600 | bytes 15212544 | tf_op jit(solution)/shard_map/dot_general | solution.py:91
  315.6 0.0 reduce-scatter.2.cloned.1.call-update
  315.6 84.5 %reduce-scatter.2.cloned.1.call-done = bf16[392,1024]{1,0:T(8,128)(2,1)} async-done(((bf16[392,8192]{1,0:T(8,128)(2,1)}), bf16[392,1024]{1,0:T(8,128)(2,1)}) %reduce-scatter.2.cloned.1.call-update) | async-done | bytes 802832 | tf_op jit(solution)/shard_map/reduce_scatter | solution.py:92
  400.1 1.0 constant_dynamic-slice_fusion
  401.1 3.1 collective-permute-start.2
  404.2 9.0 %collective-permute-done.2 = bf16[392,512]{1,0:T(8,128)(2,1)S(1)} collective-permute-done((bf16[392,512]{1,0:T(8,128)(2,1)S(1)}, bf16[392,512]{1,0:T(8,128)(2,1)S(1)}, u32[]{:S(2)}, u32[]{:S(2)}) %collective-permute-start.2) | collective-permute-done | bytes 401440 | tf_op jit(solution)/shard_map/ppermute | solution.py:23
  413.2 1.1 add_convert_fusion
  414.3 0.8 slice.63
  415.1 0.6 slice.64
  (4 shorter events, 0.1 us)
Async XLA Ops:
  7.9 60.0 %collective-permute-start = (bf16[3,2,512]{2,1,0:T(2,128)(2,1)S(1)}, bf16[3,2,512]{2,1,0:T(2,128)(2,1)S(1)}, u32[]{:S(2)}, u32[]{:S(2)}) collective-permute-start(bf16[3,2,512]{2,1,0:T(2,128)(2,1)S(1)} %slice.44), channel_id=1, source_target_pairs={{0,16},{16,32},{32,48},{48,64},{64,80},{80,96},{96,112},{112,128},... | collective-permute-start | bytes 18440 | tf_op jit(solution)/shard_map/ppermute | solution.py:15
  38.6 29.9 %copy-start = (bf16[3,384,512]{2,1,0:T(8,128)(2,1)S(1)}, bf16[3,384,512]{2,1,0:T(8,128)(2,1)}, u32[]{:S(2)}) copy-start(bf16[3,384,512]{2,1,0:T(8,128)(2,1)} %param.6) | copy-start | bytes 3538948
  67.9 0.6 copy-start.1
  70.2 5.7 %collective-permute-start.1 = (bf16[127,512]{1,0:T(8,128)(2,1)S(1)}, bf16[127,512]{1,0:T(8,128)(2,1)S(1)}, u32[]{:S(2)}, u32[]{:S(2)}) collective-permute-start(bf16[127,512]{1,0:T(8,128)(2,1)S(1)} %slice_bitcast_fusion.1), channel_id=1, source_target_pairs={{0,16},{16,32},{32,48},{48,64},{64,80},{80,96},{96,112},{112,128},... | collective-permute-start | bytes 390152 | tf_op jit(solution)/shard_map/ppermute | solution.py:15
  76.2 10.3 %copy-start.2 = (f32[512]{0:T(512)S(1)}, f32[512]{0:T(512)}, u32[]{:S(2)}) copy-start(f32[512]{0:T(512)} %param.9) | copy-start | bytes 6148
  85.1 1.8 copy-start.3
  87.9 20.9 %all-to-all-start = ((bf16[32,4,512]{2,1,0:T(4,128)(2,1)}), bf16[32,4,512]{2,1,0:T(4,128)(2,1)S(1)}, u32[]{:S(2)}, u32[]{:S(2)}) async-start(bf16[32,4,512]{2,1,0:T(4,128)(2,1)} %reshape.36), calls=%async_computation | async-start | bytes 262144 | tf_op jit(solution)/shard_map/all_to_all | solution.py:30
  113.0 191.9 %all-to-all-start.1 = ((bf16[32,512,256]{1,2,0:T(8,128)(2,1)}), bf16[32,512,256]{1,2,0:T(8,128)(2,1)}, u32[]{:S(2)}, u32[]{:S(2)}) async-start(bf16[32,512,256]{1,2,0:T(8,128)(2,1)} %stack.2), calls=%async_computation.1 | async-start | bytes 16777216 | tf_op jit(solution)/shard_map/all_to_all | solution.py:86
  119.2 280.9 %reduce-scatter.2.cloned.1.call-start = ((), (), s32[]{:S(2)}) async-start(), calls=%async_computation.3 | async-start | bytes 7225344 | tf_op jit(solution)/shard_map/reduce_scatter | solution.py:92
  401.1 12.1 %collective-permute-start.2 = (bf16[392,512]{1,0:T(8,128)(2,1)S(1)}, bf16[392,512]{1,0:T(8,128)(2,1)S(1)}, u32[]{:S(2)}, u32[]{:S(2)}) collective-permute-start(bf16[392,512]{1,0:T(8,128)(2,1)S(1)} %constant_dynamic-slice_fusion), channel_id=1, source_target_pairs={{0,1},{1,0},{2,3},{3,2},{4,5},{5,4},{6,7},{7,6},{8,9},{9,8},{10,11... | collective-permute-start | bytes 1204232 | tf_op jit(solution)/shard_map/ppermute | solution.py:23
Sparse Core Ops, SparseCore 0:
  315.7 84.3 reduce-scatter.1
